TPU v7x, 512 devices: a whole 4x4x16 slice. The times are simulated.
512 devices in a mesh: req: 64 (over y_hi, z, core), tp: 8 (over y_lo, x).
Axes of the slice: x: 4, y: 4 (y_hi: 2, y_lo: 2; y = y_hi * 2 + y_lo), z: 16, core: 2. Of those that a mesh axis runs over, the one named last changes fastest.
Arguments:
- tokens: bfloat16 [64, 512, 2048], P('req', 'tp'), may hold values from -6 to 6
- w_q: bfloat16 [2048, 1024], P(None, 'tp')
- w_k: bfloat16 [2048, 1024], P(None, 'tp')
- w_v: bfloat16 [2048, 1024], P(None, 'tp'), may hold values from -0.125 to 0.125
- w_o: bfloat16 [1024, 2048], P('tp'), may hold values from -0.1875 to 0.1875
- q_gain: float32 [1024], P('tp'), may hold values from 0.1 to 1.9
- k_gain: float32 [1024], P('tp'), may hold values from 0.1 to 1.9
- out_gain: float32 [2048], replicated, may hold values from 0.1 to 1.9
- cache_lens: int32 [64], P('req'), may hold values from 512 to 4096, as said below
- group_ids: int32 [64], replicated, may hold values from 0 to 7
- prefix_cache: bfloat16 [8, 1024, 2048], P(None, 'req', 'tp'), may hold values from -6 to 6
- cache_rows: bfloat16 [64, 4096, 2048], P('req', None, 'tp'), may hold values from -105 to 105
Outputs:
- hidden: bfloat16 [64, 512, 2048], P('req', 'tp')
- appended: bfloat16 [64, 512, 2048], P('req', None, 'tp')
Inputs may be any that keep to these rules, and one draw needn't show every extreme that they name: `cache_lens`: every draw holds a request with exactly 4096 cached positions.
All inputs are finite; a program needn't handle non-finite values.
Results may differ from a plain program's by a relative error of at most 0.013.
Values may be sent and summed in bfloat16 or wider, within the bound.
No kernel may reach another device: no remote copies, remote signals or barrier semaphores. Data moves between devices by JAX's collectives and lax.ppermute only.
A program may use at most 64 MiB of HBM per device.

v0:
```python
import jax
import jax.numpy as jnp
from jax import lax
from jax.experimental import pallas as pl
from jax.experimental.pallas import tpu as pltpu
from jax.sharding import PartitionSpec as P


HEADS = 8
HD = 128
NEW = 512


def rotate(values_in, positions):
    half_dim = values_in.shape[-1] // 2
    exponent = jnp.arange(half_dim, dtype=jnp.float32) * (-2.0 / values_in.shape[-1])
    inverse = jnp.power(jnp.float32(500000.0), exponent)
    angles = positions[:, None] * inverse[None, :]
    cosine = jnp.cos(angles)[:, None, :]
    sine_part = jnp.sin(angles)[:, None, :]
    first_half = values_in[..., :half_dim]
    second_half = values_in[..., half_dim:]
    return jnp.concatenate(
        [
            first_half * cosine - second_half * sine_part,
            second_half * cosine + first_half * sine_part,
        ],
        -1,
    )


def rms_scale(values_in, gain_vector):
    mean_sq = jnp.mean(values_in * values_in, axis=-1, keepdims=True)
    return values_in * lax.rsqrt(mean_sq + 1e-06) * gain_vector


QUERY_BLOCK = 256
KEY_BLOCK = 512


def scores_of(queries, keys):
    return lax.dot_general(
        queries, keys, (((1,), (1,)), ((), ())), preferred_element_type=jnp.float32
    ) * HD ** (-0.5)


def private_kernel(len_ref, q_ref, cache_ref, nk_ref, nv_ref, peak_ref, sum_ref, acc_ref, score_ref):
    block = pl.program_id(0)
    length = len_ref[0]
    queries = q_ref[...]
    cache_chunks = cache_ref.shape[0] // KEY_BLOCK
    row_ids = block * QUERY_BLOCK + lax.broadcasted_iota(jnp.int32, (QUERY_BLOCK, KEY_BLOCK), 0)
    col_ids = lax.broadcasted_iota(jnp.int32, (QUERY_BLOCK, KEY_BLOCK), 1)
    row_peak = None
    for chunk in range(cache_chunks + 1):
        if chunk < cache_chunks:
            part = scores_of(queries, cache_ref[pl.ds(chunk * KEY_BLOCK, KEY_BLOCK), pl.ds(0, HD)])
            if chunk > 0:
                part = jnp.where(col_ids + chunk * KEY_BLOCK < length, part, -1e30)
        else:
            part = jnp.where(col_ids <= row_ids, scores_of(queries, nk_ref[...]), -1e30)
        score_ref[:, pl.ds(chunk * KEY_BLOCK, KEY_BLOCK)] = part
        peak = jnp.max(part, -1, keepdims=True)
        row_peak = peak if row_peak is None else jnp.maximum(row_peak, peak)
    denominator = jnp.zeros((QUERY_BLOCK, 1), jnp.float32)
    weighted = jnp.zeros((QUERY_BLOCK, HD), jnp.float32)
    for chunk in range(cache_chunks + 1):
        weights = jnp.exp(score_ref[:, pl.ds(chunk * KEY_BLOCK, KEY_BLOCK)] - row_peak)
        if chunk < cache_chunks:
            values = cache_ref[pl.ds(chunk * KEY_BLOCK, KEY_BLOCK), pl.ds(HD, HD)]
        else:
            values = nv_ref[...]
        denominator = denominator + jnp.sum(weights, -1, keepdims=True)
        weighted = weighted + jnp.dot(
            weights.astype(jnp.bfloat16), values, preferred_element_type=jnp.float32
        )
    peak_ref[...] = jnp.broadcast_to(row_peak, peak_ref.shape)
    sum_ref[...] = jnp.broadcast_to(denominator, sum_ref.shape)
    acc_ref[...] = weighted


def shared_kernel(q_ref, pre_ref, peak_ref, sum_ref, acc_ref, wo_ref, out_ref, score_ref):
    queries = q_ref[...]
    prefix_chunks = pre_ref.shape[0] // KEY_BLOCK
    old_peak = peak_ref[:, :1]
    row_peak = old_peak
    for chunk in range(prefix_chunks):
        part = scores_of(queries, pre_ref[pl.ds(chunk * KEY_BLOCK, KEY_BLOCK), pl.ds(0, HD)])
        score_ref[:, pl.ds(chunk * KEY_BLOCK, KEY_BLOCK)] = part
        row_peak = jnp.maximum(row_peak, jnp.max(part, -1, keepdims=True))
    rescale = jnp.exp(old_peak - row_peak)
    denominator = sum_ref[:, :1] * rescale
    weighted = acc_ref[...] * rescale
    for chunk in range(prefix_chunks):
        weights = jnp.exp(score_ref[:, pl.ds(chunk * KEY_BLOCK, KEY_BLOCK)] - row_peak)
        denominator = denominator + jnp.sum(weights, -1, keepdims=True)
        weighted = weighted + jnp.dot(
            weights.astype(jnp.bfloat16),
            pre_ref[pl.ds(chunk * KEY_BLOCK, KEY_BLOCK), pl.ds(HD, HD)],
            preferred_element_type=jnp.float32,
        )
    attended = (weighted / denominator).astype(jnp.bfloat16)
    out_ref[...] = jnp.dot(
        attended, wo_ref[...], preferred_element_type=jnp.float32
    ).astype(out_ref.dtype)


def attend(cache_lens, queries, prefix_pairs, cache_pairs, keys_new, values_new, w_out):
    new_rows = queries.shape[0]
    whole = lambda block, *rest: (0, 0)
    rows = lambda block, *rest: (block, 0)
    grid = (new_rows // QUERY_BLOCK,)
    row_block = pl.BlockSpec((QUERY_BLOCK, HD), rows)
    state = jax.ShapeDtypeStruct((new_rows, HD), jnp.float32)
    peak, total, acc = pl.pallas_call(
        private_kernel,
        grid_spec=pltpu.PrefetchScalarGridSpec(
            num_scalar_prefetch=1,
            grid=grid,
            in_specs=[
                row_block,
                pl.BlockSpec(cache_pairs.shape, whole),
                pl.BlockSpec(keys_new.shape, whole),
                pl.BlockSpec(values_new.shape, whole),
            ],
            out_specs=[row_block, row_block, row_block],
            scratch_shapes=[
                pltpu.VMEM((QUERY_BLOCK, cache_pairs.shape[0] + KEY_BLOCK), jnp.float32)
            ],
        ),
        out_shape=[state, state, state],
        compiler_params=pltpu.CompilerParams(dimension_semantics=("arbitrary",)),
    )(cache_lens, queries, cache_pairs, keys_new, values_new)
    return pl.pallas_call(
        shared_kernel,
        grid=grid,
        in_specs=[
            row_block,
            pl.BlockSpec(prefix_pairs.shape, whole),
            row_block,
            row_block,
            row_block,
            pl.BlockSpec(w_out.shape, whole),
        ],
        out_specs=pl.BlockSpec((QUERY_BLOCK, w_out.shape[1]), rows),
        out_shape=jax.ShapeDtypeStruct((new_rows, w_out.shape[1]), jnp.bfloat16),
        scratch_shapes=[pltpu.VMEM((QUERY_BLOCK, prefix_pairs.shape[0]), jnp.float32)],
        compiler_params=pltpu.CompilerParams(dimension_semantics=("arbitrary",)),
    )(queries, prefix_pairs, peak, total, acc, w_out)


def layer(
    tokens,
    w_q,
    w_k,
    w_v,
    w_o,
    q_gain,
    k_gain,
    out_gain,
    cache_lens,
    group_ids,
    prefix_cache,
    cache_rows,
):
    heads_local = w_q.shape[1] // HD
    tp_size = lax.axis_size("tp")
    flat_rows = lax.all_to_all(
        jnp.broadcast_to(tokens, (tp_size,) + tokens.shape[1:]), "tp", 0, 0, tiled=True
    ).reshape(-1, tokens.shape[2])
    outgoing = jnp.take(prefix_cache, group_ids, axis=0)
    chosen = lax.all_to_all(outgoing, "req", 0, 0, tiled=True)
    queries = jnp.dot(flat_rows, w_q, preferred_element_type=jnp.float32)
    keys_new = jnp.dot(flat_rows, w_k, preferred_element_type=jnp.float32)
    values_new = jnp.dot(flat_rows, w_v, preferred_element_type=jnp.float32)
    square_sums = lax.psum((jnp.sum(queries * queries, -1), jnp.sum(keys_new * keys_new, -1)), "tp")
    full_width = HEADS * HD
    queries = queries * lax.rsqrt(square_sums[0] / full_width + 1e-06)[:, None] * q_gain
    keys_new = keys_new * lax.rsqrt(square_sums[1] / full_width + 1e-06)[:, None] * k_gain
    prefix_len = prefix_cache.shape[1] * lax.axis_size("req")
    length = cache_lens[0]
    positions = (prefix_len + length + jnp.arange(NEW, dtype=jnp.int32)).astype(jnp.float32)
    q_rot = rotate(queries.reshape(NEW, heads_local, HD), positions).astype(jnp.bfloat16)
    k_rot = rotate(keys_new.reshape(NEW, heads_local, HD), positions).astype(jnp.bfloat16)
    v_new = values_new.reshape(NEW, heads_local, HD).astype(jnp.bfloat16)
    appended = jnp.stack([k_rot, v_new], axis=2).reshape(1, NEW, heads_local * 2 * HD)

    shared = chosen.reshape(-1, heads_local * 2 * HD)
    cached = cache_rows[0]
    partial_sum = None
    for head in range(heads_local):
        pair = slice(head * 2 * HD, (head + 1) * 2 * HD)
        partial = attend(
            cache_lens,
            q_rot[:, head],
            shared[:, pair],
            cached[:, pair],
            k_rot[:, head],
            v_new[:, head],
            w_o[head * HD : (head + 1) * HD],
        )
        partial = partial if heads_local == 1 else partial.astype(jnp.float32)
        partial_sum = partial if partial_sum is None else partial_sum + partial
    partial_out = partial_sum.astype(jnp.bfloat16)
    blocks_out = partial_out.astype(jnp.bfloat16).reshape(tp_size, -1, partial_out.shape[1])
    received = lax.all_to_all(blocks_out, "tp", 0, 0, tiled=True)
    mine = jnp.sum(received.astype(jnp.float32), 0)
    hidden = (tokens[0].astype(jnp.float32) + rms_scale(mine, out_gain)).astype(jnp.bfloat16)[None]
    return (hidden, appended)


def solution(mesh):
    return jax.shard_map(
        layer,
        mesh=mesh,
        in_specs=(
            P("req", "tp", None),
            P(None, "tp"),
            P(None, "tp"),
            P(None, "tp"),
            P("tp", None),
            P("tp"),
            P("tp"),
            P(),
            P("req"),
            P(),
            P(None, "req", "tp"),
            P("req", None, "tp"),
        ),
        out_specs=(P("req", "tp", None), P("req", None, "tp")),
        check_vma=False,
    )
```

profile of v0, /device:TPU:1, one launch (start us, length us, event | category | flops | bytes accessed | tf_op | source)
XLA Modules:
  0.0 128.3 jit_solution(18139098498854232848)
XLA Ops:
  0.6 2.6 %broadcast_in_dim.17 = bf16[8,64,2048]{2,1,0:T(8,128)(2,1)} broadcast(bf16[64,2048]{1,0:T(8,128)(2,1)} %bitcast.45), dimensions={1,2} | broadcast | bytes 2359296 | tf_op jit(solution)/shard_map/broadcast_in_dim | solution.py:169
  3.3 6.0 %all-to-all-start = ((bf16[8,64,2048]{2,1,0:T(8,128)(2,1)}), bf16[8,64,2048]{2,1,0:T(8,128)(2,1)S(1)}, u32[]{:S(2)}, u32[]{:S(2)}) async-start(bf16[8,64,2048]{2,1,0:T(8,128)(2,1)} %broadcast_in_dim.17), calls=%async_computation | async-start | bytes 4194304 | tf_op jit(solution)/shard_map/all_to_all | solution.py:168
  9.9 0.6 gather_fusion
  10.6 0.9 broadcast_select_fusion
  11.5 24.8 %all-to-all-done = bf16[8,64,2048]{2,1,0:T(8,128)(2,1)S(1)} async-done(((bf16[8,64,2048]{2,1,0:T(8,128)(2,1)}), bf16[8,64,2048]{2,1,0:T(8,128)(2,1)S(1)}, u32[]{:S(2)}, u32[]{:S(2)}) %all-to-all-start) | async-done | bytes 2097184 | tf_op jit(solution)/shard_map/all_to_all | solution.py:168
  36.3 18.8 %all-to-all-start.1 = ((bf16[64,16,256]{2,1,0:T(8,128)(2,1)}), bf16[64,16,256]{2,1,0:T(8,128)(2,1)S(1)}, u32[]{:S(2)}, u32[]{:S(2)}) async-start(bf16[64,16,256]{2,1,0:T(8,128)(2,1)} %broadcast_select_fusion), calls=%async_computation.1 | async-start | bytes 1048576 | tf_op jit(solution)/shard_map/all_to_all | solution.py:172
  55.1 0.8 multiply_reduce_fusion.2
  56.0 0.8 copy.17
  56.8 1.9 %multiply_reduce_fusion.1 = (f32[512]{0:T(512)S(1)}, f32[512,128]{0,1:T(8,128)S(1)}) fusion(bf16[512,2048]{1,0:T(8,128)(2,1)S(1)} %bitcast.35, bf16[2048,128]{1,0:T(8,128)(2,1)} %param.14), kind=kOutput, calls=%fused_computation.29 | convolution fusion | flops 268566016 | bytes 2885632 | tf_op jit(solution)/shard_map/dot_general | solution.py:174
  58.7 0.8 copy.18
  59.6 17.5 %all-reduce = (f32[512]{0:T(512)S(1)}, f32[512]{0:T(512)S(1)}) all-reduce(f32[512]{0:T(512)S(1)} %get-tuple-element.18, f32[512]{0:T(512)S(1)} %get-tuple-element.20), channel_id=1, replica_groups=mesh['req'=64,'tp'=8] {'tp'}, use_global_device_ids=true, to_apply=%region_1.2 | all-reduce | flops 1024 | bytes 8192 | tf_op jit(solution)/shard_map/psum | solution.py:176
  77.1 1.1 multiply_bitcast_fusion.1
  78.3 1.1 multiply_bitcast_fusion
  79.3 1.3 %fusion.16 = (bf16[512,1,64]{2,0,1:T(8,128)(2,1)S(1)}, bf16[512,1,64]{2,0,1:T(8,128)(2,1)S(1)}, bf16[512,64]{1,0:T(8,128)(2,1)S(1)}, bf16[512,64]{1,0:T(8,128)(2,1)S(1)}) fusion(f32[512,1,128]{2,0,1:T(8,128)S(1)} %multiply_bitcast_fusion, f32[64]{0:T(128)S(1)} %multiply_power_fusion, f32[512]{0:T(512)S(1)} %add_convert_fusion, ...), kind=kLoop, calls=%fused_computation.24 | loop fusion | flops 557056 | bytes 788736 | tf_op jit(solution)/shard_map/convert.7
  80.6 0.8 pad_maximum_fusion.2.nk_ref
  81.4 0.8 pad_maximum_fusion.1.q_ref
  82.2 1.4 %convolution_convert_fusion.nv_ref = bf16[512,128]{1,0:T(8,128)(2,1)} fusion(bf16[512,2048]{1,0:T(8,128)(2,1)S(1)} %bitcast.36, bf16[2048,128]{1,0:T(8,128)(2,1)S(1)} %copy-done.5), kind=kOutput, calls=%fused_computation.2 | convolution fusion | flops 268500992 | bytes 2752512 | tf_op jit(solution)/shard_map/dot_general | solution.py:175
  83.5 6.8 %shard_map.131 = (f32[512,128]{1,0:T(8,128)}, f32[512,128]{1,0:T(8,128)}, f32[512,128]{1,0:T(8,128)}) custom-call(s32[1]{0:T(128)S(6)} %copy.23.len_ref, bf16[512,128]{1,0:T(8,128)(2,1)} %pad_maximum_fusion.1.q_ref, bf16[4096,256]{1,0:T(8,128)(2,1)} %bitcast.38, bf16[512,128]{1,0:T(8,128)(2,1)} %pad_maximum_fusion.2.nk_ref, ...), custom_call_target="tpu_custom_call" | custom-call | tf_op jit(solution)/shard_map/pallas_call | solution.py:115
  90.4 0.8 copy-done.2
  91.2 4.9 %shard_map.132 = bf16[512,2048]{1,0:T(8,128)(2,1)} custom-call(bf16[512,128]{1,0:T(8,128)(2,1)} %pad_maximum_fusion.1.q_ref, bf16[1024,256]{1,0:T(8,128)(2,1)} %bitcast.39, f32[512,128]{1,0:T(8,128)} %get-tuple-element.5.peak_ref, f32[512,128]{1,0:T(8,128)} %get-tuple-element.6.sum_ref, f32[512,128]{1,0:T(8,128)} %get-tuple-element.7.acc_ref, ...), custom_call_target="tpu_custom_call" | custom-call | tf_op jit(solution)/shard_map/pallas_call | solution.py:134
  96.1 3.7 %all-to-all-start.2 = ((bf16[8,64,2048]{2,1,0:T(8,128)(2,1)}), bf16[8,64,2048]{2,1,0:T(8,128)(2,1)S(1)}, u32[]{:S(2)}, u32[]{:S(2)}) async-start(bf16[8,64,2048]{2,1,0:T(8,128)(2,1)} %bitcast.37), calls=%async_computation.2 | async-start | bytes 4194304 | tf_op jit(solution)/shard_map/all_to_all | solution.py:206
  100.1 0.8 copy.21
  101.0 25.9 %all-to-all-done.2 = bf16[8,64,2048]{2,1,0:T(8,128)(2,1)S(1)} async-done(((bf16[8,64,2048]{2,1,0:T(8,128)(2,1)}), bf16[8,64,2048]{2,1,0:T(8,128)(2,1)S(1)}, u32[]{:S(2)}, u32[]{:S(2)}) %all-to-all-start.2) | async-done | bytes 2097184 | tf_op jit(solution)/shard_map/all_to_all | solution.py:206
  127.4 0.9 fusion.2
  (31 shorter events, 0.8 us)
Async XLA Ops:
  0.6 54.5 %copy-start = (bf16[2048,128]{1,0:T(8,128)(2,1)S(1)}, bf16[2048,128]{1,0:T(8,128)(2,1)}, u32[]{:S(2)}) copy-start(bf16[2048,128]{1,0:T(8,128)(2,1)} %param.13) | copy-start | bytes 1572868
  3.3 6.6 %copy-start.9 = (s32[64]{0:T(128)S(1)}, s32[64]{0:T(128)}, u32[]{:S(2)}) copy-start(s32[64]{0:T(128)} %param.21) | copy-start | bytes 772
  3.3 6.7 %copy-start.1 = (bf16[8,16,256]{2,1,0:T(8,128)(2,1)S(1)}, bf16[8,16,256]{2,1,0:T(8,128)(2,1)}, u32[]{:S(2)}) copy-start(bf16[8,16,256]{2,1,0:T(8,128)(2,1)} %param.22) | copy-start | bytes 196612
  3.3 33.1 %all-to-all-start = ((bf16[8,64,2048]{2,1,0:T(8,128)(2,1)}), bf16[8,64,2048]{2,1,0:T(8,128)(2,1)S(1)}, u32[]{:S(2)}, u32[]{:S(2)}) async-start(bf16[8,64,2048]{2,1,0:T(8,128)(2,1)} %broadcast_in_dim.17), calls=%async_computation | async-start | bytes 4194304 | tf_op jit(solution)/shard_map/all_to_all | solution.py:168
  36.3 54.0 %all-to-all-start.1 = ((bf16[64,16,256]{2,1,0:T(8,128)(2,1)}), bf16[64,16,256]{2,1,0:T(8,128)(2,1)S(1)}, u32[]{:S(2)}, u32[]{:S(2)}) async-start(bf16[64,16,256]{2,1,0:T(8,128)(2,1)} %broadcast_select_fusion), calls=%async_computation.1 | async-start | bytes 1048576 | tf_op jit(solution)/shard_map/all_to_all | solution.py:172
  56.0 21.1 %copy-start.7 = (f32[128]{0:T(128)S(1)}, f32[128]{0:T(128)}, u32[]{:S(2)}) copy-start(f32[128]{0:T(128)} %param.17) | copy-start | bytes 1540
  56.8 21.4 %copy-start.8 = (f32[128]{0:T(128)S(1)}, f32[128]{0:T(128)}, u32[]{:S(2)}) copy-start(f32[128]{0:T(128)} %param.18) | copy-start | bytes 1540
  77.1 5.1 %copy-start.5 = (bf16[2048,128]{1,0:T(8,128)(2,1)S(1)}, bf16[2048,128]{1,0:T(8,128)(2,1)}, u32[]{:S(2)}) copy-start(bf16[2048,128]{1,0:T(8,128)(2,1)} %param.15) | copy-start | bytes 1572868
  90.4 0.8 copy-start.2
  96.1 3.7 %copy-start.3 = (bf16[512,128]{1,0:T(8,128)(2,1)S(1)}, bf16[512,128]{1,0:T(8,128)(2,1)}, u32[]{:S(2)}) copy-start(bf16[512,128]{1,0:T(8,128)(2,1)} %convolution_convert_fusion.nv_ref) | copy-start | bytes 393220
  96.1 30.8 %all-to-all-start.2 = ((bf16[8,64,2048]{2,1,0:T(8,128)(2,1)}), bf16[8,64,2048]{2,1,0:T(8,128)(2,1)S(1)}, u32[]{:S(2)}, u32[]{:S(2)}) async-start(bf16[8,64,2048]{2,1,0:T(8,128)(2,1)} %bitcast.37), calls=%async_computation.2 | async-start | bytes 4194304 | tf_op jit(solution)/shard_map/all_to_all | solution.py:206
  100.0 27.4 %copy-start.4 = (bf16[1,64,2048]{2,1,0:T(8,128)(2,1)S(1)}, bf16[1,64,2048]{2,1,0:T(8,128)(2,1)}, u32[]{:S(2)}) copy-start(bf16[1,64,2048]{2,1,0:T(8,128)(2,1)} %param.12) | copy-start | bytes 786436
  100.0 27.4 %copy-start.6 = (f32[2048]{0:T(1024)S(1)}, f32[2048]{0:T(1024)}, u32[]{:S(2)}) copy-start(f32[2048]{0:T(1024)} %param.19) | copy-start | bytes 24580
where the time goes:
time: 129 us; the launch traced here: 128 us
  waiting for transfers between devices  50.7 us (39%)
  starting transfers between devices  28.5 us (22%)
  blocking collectives  17.5 us (14%)
  Pallas kernels  11.8 us (9%)
  other arithmetic  7.47 us (6%)
  local copies, waits for them, and re-layouts  6.71 us (5%)
  matrix products  4.09 us (3%)
  between operations  1.49 us (1%)
    all_to_all x1, waiting for transfers between devices, layer(): received = lax.all_to_all(blocks_out, 'tp', 0, 0, tiled=True)  25.9 us
    all_to_all x1, waiting for transfers between devices, layer(): lax.all_to_all(jnp.broadcast_to(tokens, (tp_size,) + tokens.shape[1:]), '...  24.8 us
    all_to_all x1, starting transfers between devices, layer(): chosen = lax.all_to_all(outgoing, 'req', 0, 0, tiled=True)  18.8 us
    psum x1, blocking collectives, layer(): lax.psum((jnp.sum(queries * queries, -1), jnp.sum(keys_new * keys_new, -1...  17.5 us
    pallas_call x1, Pallas kernels, attend(): pl.pallas_call(private_kernel, grid_spec=pltpu.PrefetchScalarGridSpec(num...  6.83 us
    all_to_all x1, starting transfers between devices, layer(): lax.all_to_all(jnp.broadcast_to(tokens, (tp_size,) + tokens.shape[1:]), '...  5.98 us
    pallas_call x1, Pallas kernels, attend(): pl.pallas_call(shared_kernel, grid=grid, in_specs=[row_block, pl.BlockSpe...  4.93 us
    all_to_all x1, starting transfers between devices, layer(): received = lax.all_to_all(blocks_out, 'tp', 0, 0, tiled=True)  3.73 us
  transfers between devices with their start and end apart: 3, of which 2 were waited for; matrix products, arithmetic and copies ran while one was open for 10% of the time, Pallas kernels for 5%

commit v1 on v0

--- a/solution.py
+++ b/solution.py
@@ -4,7 +4,6 @@
 from jax.experimental import pallas as pl
 from jax.experimental.pallas import tpu as pltpu
 from jax.sharding import PartitionSpec as P
-
 
 HEADS = 8
 HD = 128
@@ -44,7 +43,7 @@
     ) * HD ** (-0.5)
 
 
-def private_kernel(len_ref, q_ref, cache_ref, nk_ref, nv_ref, peak_ref, sum_ref, acc_ref, score_ref):
+def private_kernel(len_ref, q_ref, cache_ref, nk_ref, nv_ref, stat_ref, acc_ref, score_ref):
     block = pl.program_id(0)
     length = len_ref[0]
     queries = q_ref[...]
@@ -74,22 +73,22 @@
         weighted = weighted + jnp.dot(
             weights.astype(jnp.bfloat16), values, preferred_element_type=jnp.float32
         )
-    peak_ref[...] = jnp.broadcast_to(row_peak, peak_ref.shape)
-    sum_ref[...] = jnp.broadcast_to(denominator, sum_ref.shape)
+    lane = lax.broadcasted_iota(jnp.int32, stat_ref.shape, 1)
+    stat_ref[...] = jnp.where(lane == 0, row_peak, denominator)
     acc_ref[...] = weighted
 
 
-def shared_kernel(q_ref, pre_ref, peak_ref, sum_ref, acc_ref, wo_ref, out_ref, score_ref):
+def shared_kernel(q_ref, pre_ref, stat_ref, acc_ref, wo_ref, out_ref, score_ref):
     queries = q_ref[...]
     prefix_chunks = pre_ref.shape[0] // KEY_BLOCK
-    old_peak = peak_ref[:, :1]
+    old_peak = stat_ref[:, :1]
     row_peak = old_peak
     for chunk in range(prefix_chunks):
         part = scores_of(queries, pre_ref[pl.ds(chunk * KEY_BLOCK, KEY_BLOCK), pl.ds(0, HD)])
         score_ref[:, pl.ds(chunk * KEY_BLOCK, KEY_BLOCK)] = part
         row_peak = jnp.maximum(row_peak, jnp.max(part, -1, keepdims=True))
     rescale = jnp.exp(old_peak - row_peak)
-    denominator = sum_ref[:, :1] * rescale
+    denominator = stat_ref[:, 1:2] * rescale
     weighted = acc_ref[...] * rescale
     for chunk in range(prefix_chunks):
         weights = jnp.exp(score_ref[:, pl.ds(chunk * KEY_BLOCK, KEY_BLOCK)] - row_peak)
@@ -112,7 +111,7 @@
     grid = (new_rows // QUERY_BLOCK,)
     row_block = pl.BlockSpec((QUERY_BLOCK, HD), rows)
     state = jax.ShapeDtypeStruct((new_rows, HD), jnp.float32)
-    peak, total, acc = pl.pallas_call(
+    stats, acc = pl.pallas_call(
         private_kernel,
         grid_spec=pltpu.PrefetchScalarGridSpec(
             num_scalar_prefetch=1,
@@ -123,12 +122,12 @@
                 pl.BlockSpec(keys_new.shape, whole),
                 pl.BlockSpec(values_new.shape, whole),
             ],
-            out_specs=[row_block, row_block, row_block],
+            out_specs=[row_block, row_block],
             scratch_shapes=[
                 pltpu.VMEM((QUERY_BLOCK, cache_pairs.shape[0] + KEY_BLOCK), jnp.float32)
             ],
         ),
-        out_shape=[state, state, state],
+        out_shape=[state, state],
         compiler_params=pltpu.CompilerParams(dimension_semantics=("arbitrary",)),
     )(cache_lens, queries, cache_pairs, keys_new, values_new)
     return pl.pallas_call(
@@ -139,14 +138,13 @@
             pl.BlockSpec(prefix_pairs.shape, whole),
             row_block,
             row_block,
-            row_block,
             pl.BlockSpec(w_out.shape, whole),
         ],
         out_specs=pl.BlockSpec((QUERY_BLOCK, w_out.shape[1]), rows),
         out_shape=jax.ShapeDtypeStruct((new_rows, w_out.shape[1]), jnp.bfloat16),
         scratch_shapes=[pltpu.VMEM((QUERY_BLOCK, prefix_pairs.shape[0]), jnp.float32)],
         compiler_params=pltpu.CompilerParams(dimension_semantics=("arbitrary",)),
-    )(queries, prefix_pairs, peak, total, acc, w_out)
+    )(queries, prefix_pairs, stats, acc, w_out)
 
 
 def layer(
@@ -203,8 +201,7 @@
         partial_sum = partial if partial_sum is None else partial_sum + partial
     partial_out = partial_sum.astype(jnp.bfloat16)
     blocks_out = partial_out.astype(jnp.bfloat16).reshape(tp_size, -1, partial_out.shape[1])
-    received = lax.all_to_all(blocks_out, "tp", 0, 0, tiled=True)
-    mine = jnp.sum(received.astype(jnp.float32), 0)
+    mine = jnp.sum(lax.all_to_all(blocks_out, "tp", 0, 0, tiled=True).astype(jnp.float32), 0)
     hidden = (tokens[0].astype(jnp.float32) + rms_scale(mine, out_gain)).astype(jnp.bfloat16)[None]
     return (hidden, appended)
 

time: 129 us -> 130 us (level)
  no operation moved by 1% of the time
where the time goes in v1:
time: 130 us; the launch traced here: 129 us
  waiting for transfers between devices  50.7 us (39%)
  starting transfers between devices  28.5 us (22%)
  blocking collectives  17.5 us (13%)
  Pallas kernels  12.7 us (10%)
  other arithmetic  7.47 us (6%)
  local copies, waits for them, and re-layouts  6.71 us (5%)
  matrix products  4.09 us (3%)
  between operations  1.49 us (1%)
    all_to_all x1, waiting for transfers between devices, layer(): lax.all_to_all(blocks_out, 'tp', 0, 0, tiled=True).astype(jnp.float32)  25.9 us
    all_to_all x1, waiting for transfers between devices, layer(): lax.all_to_all(jnp.broadcast_to(tokens, (tp_size,) + tokens.shape[1:]), '...  24.8 us
    all_to_all x1, starting transfers between devices, layer(): chosen = lax.all_to_all(outgoing, 'req', 0, 0, tiled=True)  18.8 us
    psum x1, blocking collectives, layer(): lax.psum((jnp.sum(queries * queries, -1), jnp.sum(keys_new * keys_new, -1...  17.5 us
    pallas_call x1, Pallas kernels, attend(): pl.pallas_call(private_kernel, grid_spec=pltpu.PrefetchScalarGridSpec(num...  6.83 us
    all_to_all x1, starting transfers between devices, layer(): lax.all_to_all(jnp.broadcast_to(tokens, (tp_size,) + tokens.shape[1:]), '...  5.98 us
    pallas_call x1, Pallas kernels, attend(): pl.pallas_call(shared_kernel, grid=grid, in_specs=[row_block, pl.BlockSpe...  5.86 us
    all_to_all x1, starting transfers between devices, layer(): lax.all_to_all(blocks_out, 'tp', 0, 0, tiled=True).astype(jnp.float32)  3.73 us
  transfers between devices with their start and end apart: 3, of which 2 were waited for; matrix products, arithmetic and copies ran while one was open for 10% of the time, Pallas kernels for 5%

profile of v1, /device:TPU:1, one launch (start us, length us, event | category | flops | bytes accessed | tf_op | source)
XLA Modules:
  0.0 129.2 jit_solution(18399198711468021773)
XLA Ops:
  0.6 2.6 %broadcast_in_dim.17 = bf16[8,64,2048]{2,1,0:T(8,128)(2,1)} broadcast(bf16[64,2048]{1,0:T(8,128)(2,1)} %bitcast.45), dimensions={1,2} | broadcast | bytes 2359296 | tf_op jit(solution)/shard_map/broadcast_in_dim | solution.py:167
  3.3 6.0 %all-to-all-start = ((bf16[8,64,2048]{2,1,0:T(8,128)(2,1)}), bf16[8,64,2048]{2,1,0:T(8,128)(2,1)S(1)}, u32[]{:S(2)}, u32[]{:S(2)}) async-start(bf16[8,64,2048]{2,1,0:T(8,128)(2,1)} %broadcast_in_dim.17), calls=%async_computation | async-start | bytes 4194304 | tf_op jit(solution)/shard_map/all_to_all | solution.py:166
  9.9 0.6 gather_fusion
  10.6 0.9 broadcast_select_fusion
  11.5 24.8 %all-to-all-done = bf16[8,64,2048]{2,1,0:T(8,128)(2,1)S(1)} async-done(((bf16[8,64,2048]{2,1,0:T(8,128)(2,1)}), bf16[8,64,2048]{2,1,0:T(8,128)(2,1)S(1)}, u32[]{:S(2)}, u32[]{:S(2)}) %all-to-all-start) | async-done | bytes 2097184 | tf_op jit(solution)/shard_map/all_to_all | solution.py:166
  36.3 18.8 %all-to-all-start.1 = ((bf16[64,16,256]{2,1,0:T(8,128)(2,1)}), bf16[64,16,256]{2,1,0:T(8,128)(2,1)S(1)}, u32[]{:S(2)}, u32[]{:S(2)}) async-start(bf16[64,16,256]{2,1,0:T(8,128)(2,1)} %broadcast_select_fusion), calls=%async_computation.1 | async-start | bytes 1048576 | tf_op jit(solution)/shard_map/all_to_all | solution.py:170
  55.1 0.8 multiply_reduce_fusion.2
  56.0 0.8 copy.17
  56.8 1.9 %multiply_reduce_fusion.1 = (f32[512]{0:T(512)S(1)}, f32[512,128]{0,1:T(8,128)S(1)}) fusion(bf16[512,2048]{1,0:T(8,128)(2,1)S(1)} %bitcast.35, bf16[2048,128]{1,0:T(8,128)(2,1)} %param.14), kind=kOutput, calls=%fused_computation.29 | convolution fusion | flops 268566016 | bytes 2885632 | tf_op jit(solution)/shard_map/dot_general | solution.py:172
  58.7 0.8 copy.18
  59.6 17.5 %all-reduce = (f32[512]{0:T(512)S(1)}, f32[512]{0:T(512)S(1)}) all-reduce(f32[512]{0:T(512)S(1)} %get-tuple-element.16, f32[512]{0:T(512)S(1)} %get-tuple-element.18), channel_id=1, replica_groups=mesh['req'=64,'tp'=8] {'tp'}, use_global_device_ids=true, to_apply=%region_1.2 | all-reduce | flops 1024 | bytes 8192 | tf_op jit(solution)/shard_map/psum | solution.py:174
  77.1 1.1 multiply_bitcast_fusion.1
  78.3 1.1 multiply_bitcast_fusion
  79.3 1.3 fusion.16
  80.6 0.8 pad_maximum_fusion.2.nk_ref
  81.4 0.8 pad_maximum_fusion.1.q_ref
  82.2 1.4 %convolution_convert_fusion.nv_ref = bf16[512,128]{1,0:T(8,128)(2,1)} fusion(bf16[512,2048]{1,0:T(8,128)(2,1)S(1)} %bitcast.36, bf16[2048,128]{1,0:T(8,128)(2,1)S(1)} %copy-done.5), kind=kOutput, calls=%fused_computation.2 | convolution fusion | flops 268500992 | bytes 2752512 | tf_op jit(solution)/shard_map/dot_general | solution.py:173
  83.5 6.8 %shard_map.131 = (f32[512,128]{1,0:T(8,128)}, f32[512,128]{1,0:T(8,128)}) custom-call(s32[1]{0:T(128)S(6)} %copy.23.len_ref, bf16[512,128]{1,0:T(8,128)(2,1)} %pad_maximum_fusion.1.q_ref, bf16[4096,256]{1,0:T(8,128)(2,1)} %bitcast.38, bf16[512,128]{1,0:T(8,128)(2,1)} %pad_maximum_fusion.2.nk_ref, bf16[512,128]{1,0:T(8,128)(2,1)} %convolution_convert_fusion.nv_ref), custom_call_target="tpu_custom_call" | custom-call | tf_op jit(solution)/shard_map/pallas_call | solution.py:114
  90.4 0.8 copy-done.2
  91.2 5.9 %shard_map.132 = bf16[512,2048]{1,0:T(8,128)(2,1)} custom-call(bf16[512,128]{1,0:T(8,128)(2,1)} %pad_maximum_fusion.1.q_ref, bf16[1024,256]{1,0:T(8,128)(2,1)} %bitcast.39, f32[512,128]{1,0:T(8,128)} %get-tuple-element.4.stat_ref, f32[512,128]{1,0:T(8,128)} %get-tuple-element.5.acc_ref, bf16[128,2048]{1,0:T(8,128)(2,1)} %wo_ref.1), custom_call_target="tpu_custom_call" | custom-call | tf_op jit(solution)/shard_map/pallas_call | solution.py:133
  97.0 3.7 %all-to-all-start.2 = ((bf16[8,64,2048]{2,1,0:T(8,128)(2,1)}), bf16[8,64,2048]{2,1,0:T(8,128)(2,1)S(1)}, u32[]{:S(2)}, u32[]{:S(2)}) async-start(bf16[8,64,2048]{2,1,0:T(8,128)(2,1)} %bitcast.37), calls=%async_computation.2 | async-start | bytes 4194304 | tf_op jit(solution)/shard_map/all_to_all | solution.py:204
  101.1 0.8 copy.21
  101.9 25.9 %all-to-all-done.2 = bf16[8,64,2048]{2,1,0:T(8,128)(2,1)S(1)} async-done(((bf16[8,64,2048]{2,1,0:T(8,128)(2,1)}), bf16[8,64,2048]{2,1,0:T(8,128)(2,1)S(1)}, u32[]{:S(2)}, u32[]{:S(2)}) %all-to-all-start.2) | async-done | bytes 2097184 | tf_op jit(solution)/shard_map/all_to_all | solution.py:204
  128.3 0.9 fusion.2
  (31 shorter events, 0.8 us)
Async XLA Ops:
  0.6 54.5 %copy-start = (bf16[2048,128]{1,0:T(8,128)(2,1)S(1)}, bf16[2048,128]{1,0:T(8,128)(2,1)}, u32[]{:S(2)}) copy-start(bf16[2048,128]{1,0:T(8,128)(2,1)} %param.13) | copy-start | bytes 1572868
  3.3 6.6 %copy-start.9 = (s32[64]{0:T(128)S(1)}, s32[64]{0:T(128)}, u32[]{:S(2)}) copy-start(s32[64]{0:T(128)} %param.21) | copy-start | bytes 772
  3.3 6.7 %copy-start.1 = (bf16[8,16,256]{2,1,0:T(8,128)(2,1)S(1)}, bf16[8,16,256]{2,1,0:T(8,128)(2,1)}, u32[]{:S(2)}) copy-start(bf16[8,16,256]{2,1,0:T(8,128)(2,1)} %param.22) | copy-start | bytes 196612
  3.3 33.1 %all-to-all-start = ((bf16[8,64,2048]{2,1,0:T(8,128)(2,1)}), bf16[8,64,2048]{2,1,0:T(8,128)(2,1)S(1)}, u32[]{:S(2)}, u32[]{:S(2)}) async-start(bf16[8,64,2048]{2,1,0:T(8,128)(2,1)} %broadcast_in_dim.17), calls=%async_computation | async-start | bytes 4194304 | tf_op jit(solution)/shard_map/all_to_all | solution.py:166
  36.3 54.0 %all-to-all-start.1 = ((bf16[64,16,256]{2,1,0:T(8,128)(2,1)}), bf16[64,16,256]{2,1,0:T(8,128)(2,1)S(1)}, u32[]{:S(2)}, u32[]{:S(2)}) async-start(bf16[64,16,256]{2,1,0:T(8,128)(2,1)} %broadcast_select_fusion), calls=%async_computation.1 | async-start | bytes 1048576 | tf_op jit(solution)/shard_map/all_to_all | solution.py:170
  56.0 21.1 %copy-start.7 = (f32[128]{0:T(128)S(1)}, f32[128]{0:T(128)}, u32[]{:S(2)}) copy-start(f32[128]{0:T(128)} %param.17) | copy-start | bytes 1540
  56.8 21.4 %copy-start.8 = (f32[128]{0:T(128)S(1)}, f32[128]{0:T(128)}, u32[]{:S(2)}) copy-start(f32[128]{0:T(128)} %param.18) | copy-start | bytes 1540
  77.1 5.1 %copy-start.5 = (bf16[2048,128]{1,0:T(8,128)(2,1)S(1)}, bf16[2048,128]{1,0:T(8,128)(2,1)}, u32[]{:S(2)}) copy-start(bf16[2048,128]{1,0:T(8,128)(2,1)} %param.15) | copy-start | bytes 1572868
  90.4 0.8 copy-start.2
  97.0 3.7 %copy-start.3 = (bf16[512,128]{1,0:T(8,128)(2,1)S(1)}, bf16[512,128]{1,0:T(8,128)(2,1)}, u32[]{:S(2)}) copy-start(bf16[512,128]{1,0:T(8,128)(2,1)} %convolution_convert_fusion.nv_ref) | copy-start | bytes 393220
  97.0 30.8 %all-to-all-start.2 = ((bf16[8,64,2048]{2,1,0:T(8,128)(2,1)}), bf16[8,64,2048]{2,1,0:T(8,128)(2,1)S(1)}, u32[]{:S(2)}, u32[]{:S(2)}) async-start(bf16[8,64,2048]{2,1,0:T(8,128)(2,1)} %bitcast.37), calls=%async_computation.2 | async-start | bytes 4194304 | tf_op jit(solution)/shard_map/all_to_all | solution.py:204
  100.9 27.4 %copy-start.4 = (bf16[1,64,2048]{2,1,0:T(8,128)(2,1)S(1)}, bf16[1,64,2048]{2,1,0:T(8,128)(2,1)}, u32[]{:S(2)}) copy-start(bf16[1,64,2048]{2,1,0:T(8,128)(2,1)} %param.12) | copy-start | bytes 786436
  100.9 27.4 %copy-start.6 = (f32[2048]{0:T(1024)S(1)}, f32[2048]{0:T(1024)}, u32[]{:S(2)}) copy-start(f32[2048]{0:T(1024)} %param.19) | copy-start | bytes 24580
